TPU v7x, 128 devices: a whole 4x4x4 slice. The times are simulated.
128 devices in a mesh: leaf: 16 (over y, z), ctx: 8 (over x, core).
Axes of the slice: x: 4, y: 4, z: 4, core: 2. Of those that a mesh axis runs over, the one named last changes fastest.
Arguments:
- query_key_value_rows: bfloat16 [16384, 7168], P(('leaf', 'ctx')), may hold values from -6 to 6
- cotangent: bfloat16 [16384, 5120], P(('leaf', 'ctx')), may hold values from -6 to 6
- out_weight: bfloat16 [5120, 5120], P('ctx'), may hold values from -0.078125 to 0.078125
- parents: int32 [16, 8], P('leaf'), may hold values from 0 to 6, as said below
- rollout_spans: int32 [16384], P('leaf'), may hold values from 64 to 4096
Outputs:
- qkv_grad: bfloat16 [16384, 7168], P(('leaf', 'ctx'))
- weight_grad: bfloat16 [5120, 5120], P('ctx')
Inputs may be any that keep to these rules, and one draw needn't show every extreme that they name: parents[t, 0] = 0, every later block's parent is an earlier block of the same tree, and the last block's parent is the block just before it.
All inputs are finite; a program needn't handle non-finite values.
Results may differ from a plain program's by a relative error of at most 0.012.
The roundings to bfloat16 on the way count: a program that leaves them out, or rounds other values in their place, can miss the bound.
Values may be sent and summed in bfloat16 or wider, within the bound.
No kernel may reach another device: no remote copies, remote signals or barrier semaphores. Data moves between devices by JAX's collectives and lax.ppermute only.
A program may use at most 192 MiB of HBM per device.

v0:
```python
import math
import jax
import jax.numpy as jnp
from jax import lax
from jax.sharding import PartitionSpec as P

QUERY_HEADS = 40
KEY_VALUE_HEADS = 8
HEAD_SIZE = 128
BLK = 128
log_base = 1024.0


def ancestors(parents):
    number = parents.shape[0]
    indices = jnp.arange(number, dtype=jnp.int32)

    def advance(iteration, state):
        current, reached = state
        current = jnp.sum(
            jnp.where(current[:, None] == indices[None, :], parents[None, :], 0), axis=1
        )
        return (current, reached | (current[:, None] == indices[None, :]))

    return lax.fori_loop(0, number, advance, (indices, indices[:, None] == indices[None, :]))[1]


def token_mask(reached, first_row, query_count, key_count):
    query_pos = first_row + jnp.arange(query_count, dtype=jnp.int32)
    key_pos = jnp.arange(key_count, dtype=jnp.int32)
    block_part = reached[first_row // BLK : (first_row + query_count) // BLK, : key_count // BLK]
    expanded = jnp.repeat(jnp.repeat(block_part, BLK, axis=0), BLK, axis=1)
    same_block = (query_pos // BLK)[:, None] == (key_pos // BLK)[None, :]
    return expanded & (jnp.logical_not(same_block) | (key_pos[None, :] <= query_pos[:, None]))


def span_softness(rollout_spans):
    return jnp.log(rollout_spans.astype(jnp.float32)) * (
        1.0 / (math.log(log_base) * math.sqrt(HEAD_SIZE))
    )


def contract_rows(left, right):
    return lax.dot_general(
        left, right, (((0,), (0,)), ((), ())), preferred_element_type=jnp.float32
    )


def contract_cols(left, right):
    return lax.dot_general(
        left, right, (((1,), (1,)), ((), ())), preferred_element_type=jnp.float32
    )


def local(query_key_value_rows, cotangent, out_weight, parents, rollout_spans):
    queries_per_group = QUERY_HEADS // KEY_VALUE_HEADS
    head_rows = lax.all_to_all(query_key_value_rows, "ctx", split_axis=1, concat_axis=0, tiled=True)
    tree_len = head_rows.shape[0]
    kv_local = head_rows.shape[1] // ((queries_per_group + 2) * HEAD_SIZE)
    heads_local = kv_local * queries_per_group
    grouped = head_rows.reshape(tree_len, kv_local, queries_per_group + 2, HEAD_SIZE)
    asking_matrix = grouped[:, :, :queries_per_group]
    lookup_matrix = grouped[:, :, queries_per_group]
    value_rows = grouped[:, :, queries_per_group + 1]
    softness_multiplier = span_softness(rollout_spans)
    reached = ancestors(parents[0])
    block_len = min(512, tree_len)
    block_total = tree_len // block_len
    masks = []
    total_parts = []
    attended_parts = []
    for block_id in range(block_total):
        opening_slot = block_id * block_len
        closing_slot = opening_slot + block_len
        allowed = token_mask(reached, opening_slot, block_len, closing_slot)
        masks.append(allowed)
        attention_logits = jnp.einsum(
            "zpyr,kpr->pyzk",
            asking_matrix[opening_slot:closing_slot],
            lookup_matrix[:closing_slot],
            preferred_element_type=jnp.float32,
        )
        attention_logits = jnp.where(
            allowed[None, None],
            attention_logits * softness_multiplier[opening_slot:closing_slot][None, None, :, None],
            -jnp.inf,
        )
        peak_score = jnp.max(attention_logits, axis=-1, keepdims=True)
        log_total = peak_score + jnp.log(
            jnp.sum(jnp.exp(attention_logits - peak_score), axis=-1, keepdims=True)
        )
        weights_low = jnp.exp(attention_logits - log_total).astype(jnp.bfloat16)
        attended_parts.append(
            jnp.einsum(
                "gjts,sgd->tgjd",
                weights_low,
                value_rows[:closing_slot],
                preferred_element_type=jnp.float32,
            ).astype(jnp.bfloat16)
        )
        total_parts.append(log_total[..., 0])
    attended = jnp.concatenate(attended_parts, axis=0)
    log_totals = jnp.concatenate(total_parts, axis=2)
    flat_out = attended.reshape(tree_len, heads_local * HEAD_SIZE)
    shard_rows = lax.all_gather(cotangent, "ctx", axis=0, tiled=True)
    weight_low = contract_rows(flat_out, shard_rows).astype(jnp.bfloat16)
    asking_heads = jnp.transpose(asking_matrix.reshape(tree_len, heads_local, HEAD_SIZE), (1, 0, 2))
    attended_heads = jnp.transpose(attended.reshape(tree_len, heads_local, HEAD_SIZE), (1, 0, 2))
    (
        weight_low,
        shard_rows,
        masks,
        asking_heads,
        attended_heads,
        lookup_matrix,
        value_rows,
        log_totals,
    ) = lax.optimization_barrier(
        (
            weight_low,
            shard_rows,
            masks,
            asking_heads,
            attended_heads,
            lookup_matrix,
            value_rows,
            log_totals,
        )
    )
    weight_total = lax.psum(weight_low, "leaf")

    def backward_part():
        output_gradient = contract_cols(shard_rows, out_weight).astype(jnp.bfloat16)
        grad_heads = jnp.transpose(
            output_gradient.reshape(tree_len, heads_local, HEAD_SIZE), (1, 0, 2)
        )
        totals_heads = log_totals.reshape(heads_local, tree_len)

        def one_head(head_id, carry):
            key_acc, value_acc, query_grad = carry
            kv_id = head_id // queries_per_group
            keys_all = lax.dynamic_index_in_dim(lookup_matrix, kv_id, axis=1, keepdims=False)
            values_all = lax.dynamic_index_in_dim(value_rows, kv_id, axis=1, keepdims=False)
            query_all = lax.dynamic_index_in_dim(asking_heads, head_id, axis=0, keepdims=False)
            grad_all = lax.dynamic_index_in_dim(grad_heads, head_id, axis=0, keepdims=False)
            own_all = lax.dynamic_index_in_dim(attended_heads, head_id, axis=0, keepdims=False)
            totals_all = lax.dynamic_index_in_dim(totals_heads, head_id, axis=0, keepdims=False)
            key_now = lax.dynamic_index_in_dim(key_acc, kv_id, axis=1, keepdims=False)
            value_now = lax.dynamic_index_in_dim(value_acc, kv_id, axis=1, keepdims=False)
            query_blocks = []
            for block_id in range(block_total):
                opening_slot = block_id * block_len
                closing_slot = opening_slot + block_len
                query_now = query_all[opening_slot:closing_slot]
                keys_now = keys_all[:closing_slot]
                values_now = values_all[:closing_slot]
                line_multiplier = softness_multiplier[opening_slot:closing_slot][:, None]
                attention_logits = jnp.where(
                    masks[block_id], contract_cols(query_now, keys_now) * line_multiplier, -jnp.inf
                )
                attention_probabilities = jnp.exp(
                    attention_logits - totals_all[opening_slot:closing_slot][:, None]
                )
                grad_rows = grad_all[opening_slot:closing_slot]
                own_rows = own_all[opening_slot:closing_slot]
                probability_cotangent = contract_cols(grad_rows, values_now)
                middle_point = jnp.sum(
                    grad_rows.astype(jnp.float32) * own_rows.astype(jnp.float32), axis=1
                )
                logit_cotangent = (
                    attention_probabilities
                    * (probability_cotangent - middle_point[:, None])
                    * line_multiplier
                ).astype(jnp.bfloat16)
                query_blocks.append(
                    jnp.dot(logit_cotangent, keys_now, preferred_element_type=jnp.float32).astype(
                        jnp.bfloat16
                    )
                )
                key_now = key_now.at[:closing_slot].add(contract_rows(logit_cotangent, query_now))
                value_now = value_now.at[:closing_slot].add(
                    contract_rows(attention_probabilities.astype(jnp.bfloat16), grad_rows)
                )
            key_acc = lax.dynamic_update_index_in_dim(key_acc, key_now, kv_id, axis=1)
            value_acc = lax.dynamic_update_index_in_dim(value_acc, value_now, kv_id, axis=1)
            query_grad = lax.dynamic_update_index_in_dim(
                query_grad, jnp.concatenate(query_blocks, axis=0), head_id, axis=0
            )
            return (key_acc, value_acc, query_grad)

        key_acc, value_acc, query_grad = lax.fori_loop(
            0,
            heads_local,
            one_head,
            (
                jnp.zeros((tree_len, kv_local, HEAD_SIZE), jnp.float32),
                jnp.zeros((tree_len, kv_local, HEAD_SIZE), jnp.float32),
                jnp.zeros((heads_local, tree_len, HEAD_SIZE), jnp.bfloat16),
            ),
        )
        query_grad = jnp.transpose(query_grad, (1, 0, 2)).reshape(
            tree_len, kv_local, queries_per_group, HEAD_SIZE
        )
        gradients = jnp.concatenate(
            [
                query_grad,
                key_acc.astype(jnp.bfloat16)[:, :, None],
                value_acc.astype(jnp.bfloat16)[:, :, None],
            ],
            axis=2,
        )
        gradients = gradients.reshape(tree_len, kv_local * (queries_per_group + 2) * HEAD_SIZE)
        return gradients

    def no_part():
        return jnp.zeros((tree_len, kv_local * (queries_per_group + 2) * HEAD_SIZE), jnp.bfloat16)

    gradients = lax.cond(lax.axis_index("ctx") >= 0, backward_part, no_part)
    returned = lax.all_to_all(gradients, "ctx", split_axis=0, concat_axis=1, tiled=True)
    return (returned, weight_total)


def solution(mesh):
    placed = (
        P(("leaf", "ctx"), None),
        P(("leaf", "ctx"), None),
        P("ctx", None),
        P("leaf", None),
        P("leaf"),
    )
    return jax.shard_map(
        local,
        mesh=mesh,
        in_specs=placed,
        out_specs=(P(("leaf", "ctx"), None), P("ctx", None)),
        check_vma=False,
    )
```

profile of v0, /device:TPU:1, one launch (start us, length us, event | category | flops | bytes accessed | tf_op | source)
XLA Modules:
  0.0 235.3 jit_solution(3943057925726047068)
XLA Ops:
  7.9 3.9 %copy.59 = bf16[128,7168]{0,1:T(8,128)(2,1)} copy(bf16[128,7168]{1,0:T(8,128)(2,1)} %param.23) | data formatting | bytes 3670016 | tf_op args[0]
  11.8 5.9 %all-to-all-start = ((bf16[128,8,896]{0,2,1:T(8,128)(2,1)}), bf16[128,8,896]{0,2,1:T(8,128)(2,1)S(1)}, u32[]{:S(2)}, u32[]{:S(2)}) async-start(bf16[128,8,896]{0,2,1:T(8,128)(2,1)} %bitcast.310), calls=%async_computation | async-start | bytes 3670016 | tf_op jit(solution)/shard_map/all_to_all | solution.py:57
  17.7 2.2 while.53
  26.5 27.9 %all-to-all-done = bf16[128,8,896]{0,2,1:T(8,128)(2,1)S(1)} async-done(((bf16[128,8,896]{0,2,1:T(8,128)(2,1)}), bf16[128,8,896]{0,2,1:T(8,128)(2,1)S(1)}, u32[]{:S(2)}, u32[]{:S(2)}) %all-to-all-start) | async-done | bytes 1835040 | tf_op jit(solution)/shard_map/all_to_all | solution.py:57
  54.4 2.4 %copy.60 = bf16[8,128,896]{1,0,2:T(8,128)(2,1)} copy(bf16[8,128,896]{1,2,0:T(8,128)(2,1)S(1)} %bitcast.309) | data formatting | bytes 3670016 | tf_op jit(solution)/shard_map/all_to_all | solution.py:57
  56.8 2.9 %reshape.557 = bf16[1024,1,7,128]{0,3,2,1:T(8,128)(2,1)S(1)} reshape(bf16[8,128,896]{1,0,2:T(8,128)(2,1)} %copy.60) | data formatting | bytes 3670016 | tf_op jit(solution)/shard_map/reshape | solution.py:61
  64.0 1.8 fusion.34
  65.8 2.2 exponential_reduce_fusion
  68.0 1.9 fusion.55
  69.9 3.7 %fusion.52 = bf16[512,1,5,128]{3,0,2,1:T(8,128)(2,1)S(1)} fusion(f32[1024,512,5]{1,0,2:T(8,128)S(1)} %get-tuple-element.624, f32[5,512]{1,0:T(8,128)S(1)} %log_add_fusion, f32[512]{0:T(512)S(1)} %get-tuple-element.622, pred[512,1024]{0,1:T(8,128)(4,1)S(1)} %copy-done.1, bf16[1024,1,7,128]{0,3,2,1:T(8,128)(2,1)S(1)} %reshape.557), kind=kOutput, calls=%fused_computation.85 | convolution fusion | flops 681902080 | bytes 11945984 | tf_op jit(solution)/shard_map/gjts,sgd->tgjd/dot_general | solution.py:94
  73.6 1.9 fusion.77
  75.5 2.5 %copy.70 = bf16[1024,1,5,128]{0,3,2,1:T(8,128)(2,1)} copy(bf16[1024,1,5,128]{3,0,2,1:T(8,128)(2,1)} %get-tuple-element.620) | data formatting | bytes 2621440 | tf_op jit(solution)/shard_map/concatenate | solution.py:102
  79.1 6.5 %all-gather.2.cloned.1.call-done = bf16[1024,5120]{1,0:T(8,128)(2,1)} async-done(((bf16[128,5120]{1,0:T(8,128)(2,1)}), bf16[1024,5120]{1,0:T(8,128)(2,1)}) %all-gather.2.cloned.1.call-update) | async-done | bytes 10485776 | tf_op jit(solution)/shard_map/all_gather | solution.py:105
  85.6 11.7 %convolution_convert_fusion.3 = bf16[640,5120]{1,0:T(8,128)(2,1)} fusion(bf16[1024,640]{0,1:T(8,128)(2,1)} %bitcast.316, bf16[1024,5120]{1,0:T(8,128)(2,1)} %all-gather.2.cloned.1.call-done), kind=kOutput, calls=%fused_computation.66 | convolution fusion | flops 6714163200 | bytes 18350080 | tf_op jit(solution)/shard_map/dot_general | solution.py:44
  97.4 85.4 %conditional.1 = (bf16[1024,896]{0,1:T(8,128)(2,1)S(1)}) conditional(s32[]{:T(128)} %convert_element_type.154, () %tuple.93, (bf16[1024,5120]{1,0:T(8,128)(2,1)}, bf16[640,5120]{1,0:T(8,128)(2,1)}, f32[1,5,1024]{2,1,0:T(8,128)S(1)}, bf16[5,1024,128]{1,2,0:T(8,128)(2,1)}, bf16[1024,1,128]{2,0,1:T(8,128)(2,1)S(1)}, /*index=5*/f32[1024]{0:T(1024)S(1)}, ...), branch_computations={%region_7.8_spmd, %region_8.13_spmd} | conditional | flops 7727873024 | bytes 52072836 | solution.py:218
  97.4 11.6 %convolution_convert_fusion.2 = bf16[1024,640]{0,1:T(8,128)(2,1)S(1)} fusion(bf16[1024,5120]{1,0:T(8,128)(2,1)} %get-tuple-element.479, bf16[640,5120]{1,0:T(8,128)(2,1)} %get-tuple-element.510), kind=kOutput, calls=%fused_computation.54 | convolution fusion | flops 6711541760 | bytes 18350080 | tf_op jit(solution)/shard_map/cond/branch_1_fun/dot_general | solution.py:50
  110.5 70.4 %while.52 = (s32[]{:T(128)}, f32[1024,1,128]{2,0,1:T(8,128)S(1)}, f32[1024,1,128]{2,0,1:T(8,128)S(1)}, bf16[5,1024,128]{1,2,0:T(8,128)(2,1)}, bf16[5,1024,128]{1...) while((s32[]{:T(128)}, f32[1024,1,128]{2,0,1:T(8,128)S(1)}, ...), condition=%wide.region_12.12_spmd, body=%wide.region_9.11_spmd.sunk | while | flops 1014496256 | bytes 24809708 | solution.py:191
  117.5 1.6 subtract_exponential_fusion.2
  184.0 3.1 %copy.72 = bf16[1024,896]{1,0:T(8,128)(2,1)S(1)} copy(bf16[1024,896]{0,1:T(8,128)(2,1)} %copy-done) | data formatting | bytes 3670016 | tf_op jit(solution)/shard_map/cond | solution.py:218
  187.0 27.0 %all_to_all.35 = bf16[8,128,896]{2,1,0:T(8,128)(2,1)} all-to-all(bf16[8,128,896]{2,1,0:T(8,128)(2,1)S(1)} %bitcast.311), channel_id=1, replica_groups=mesh['leaf'=16,'ctx'=8] {'ctx'}, dimensions={0} | all-to-all | bytes 3670016 | tf_op jit(solution)/shard_map/all_to_all | solution.py:219
  214.0 3.2 %copy.73 = bf16[8,128,896]{1,2,0:T(8,128)(2,1)S(1)} copy(bf16[8,128,896]{2,1,0:T(8,128)(2,1)} %all_to_all.35) | data formatting | bytes 3670016 | tf_op jit(solution)/shard_map/all_to_all | solution.py:219
  217.2 2.9 %copy.74 = bf16[128,7168]{1,0:T(8,128)(2,1)} copy(bf16[128,7168]{0,1:T(8,128)(2,1)S(1)} %bitcast.312) | data formatting | bytes 3670016
  220.1 2.3 all-reduce.2.cloned.1.call-done
  222.4 6.1 %copy.127 = bf16[640,5120]{1,0:T(8,128)(2,1)} copy(bf16[640,5120]{1,0:T(8,128)(2,1)} %all-reduce.2.cloned.1.call-done) | data formatting | bytes 13107200
  (158 shorter events, 87.6 us)
Async XLA Ops:
  7.2 78.5 %all-gather.2.cloned.1.call-start = ((), (), s32[]{:S(2)}) async-start(), calls=%async_computation.2 | async-start | bytes 11796480 | tf_op jit(solution)/shard_map/all_gather | solution.py:105
  11.8 6.0 %copy-start.3 = (s32[1,8]{1,0:T(1,128)S(1)}, s32[1,8]{1,0:T(1,128)}, u32[]{:S(2)}) copy-start(s32[1,8]{1,0:T(1,128)} %param.26) | copy-start | bytes 100
  11.8 42.6 %all-to-all-start = ((bf16[128,8,896]{0,2,1:T(8,128)(2,1)}), bf16[128,8,896]{0,2,1:T(8,128)(2,1)S(1)}, u32[]{:S(2)}, u32[]{:S(2)}) async-start(bf16[128,8,896]{0,2,1:T(8,128)(2,1)} %bitcast.310), calls=%async_computation | async-start | bytes 3670016 | tf_op jit(solution)/shard_map/all_to_all | solution.py:57
  17.7 204.7 %all-reduce.2.cloned.1.call-start = ((), (), s32[]{:S(2)}) async-start(), calls=%async_computation.3 | async-start | bytes 13107200 | tf_op jit(solution)/shard_map/psum | solution.py:130
  20.0 6.5 %copy-start.2 = (s32[1024]{0:T(1024)S(1)}, s32[1024]{0:T(1024)}, u32[]{:S(2)}) copy-start(s32[1024]{0:T(1024)} %param.27) | copy-start | bytes 12292
  62.8 1.2 copy-start.1
  182.7 1.2 copy-start
Sparse Core Ops, SparseCore 0:
  9.7 75.9 all-gather.1
  97.5 124.8 all-reduce.1
where the time goes:
time: 237 us; the launch traced here: 235 us
  matrix products  89.8 us (38%)
  local copies, waits for them, and re-layouts  43.5 us (18%)
  waiting for transfers between devices  37.4 us (16%)
  blocking collectives  27 us (11%)
  other arithmetic  16.8 us (7%)
  between operations  14.2 us (6%)
  starting transfers between devices  5.97 us (3%)
    dot_general x21, matrix products, contract_cols(): lax.dot_general(left, right, (((1,), (1,)), ((), ())), preferred_element_...  39.5 us
    dot_general x21, matrix products, contract_rows(): lax.dot_general(left, right, (((0,), (0,)), ((), ())), preferred_element_...  38.2 us
    all_to_all x1, waiting for transfers between devices, local(): lax.all_to_all(query_key_value_rows, 'ctx', split_axis=1, concat_axis=0,...  27.9 us
    all_to_all x1, blocking collectives, local(): lax.all_to_all(gradients, 'ctx', split_axis=0, concat_axis=1, tiled=True)  27 us
    unnamed x13, local copies, waits for them, and re-layouts  15.4 us
    reduce_sum x5, other arithmetic, one_head(): jnp.sum(grad_rows.astype(jnp.float32) * own_rows.astype(jnp.float32), axi...  6.59 us
    all_gather x1, waiting for transfers between devices, local(): shard_rows = lax.all_gather(cotangent, 'ctx', axis=0, tiled=True)  6.48 us
    all_to_all x1, starting transfers between devices, local(): lax.all_to_all(query_key_value_rows, 'ctx', split_axis=1, concat_axis=0,...  5.93 us
  transfers between devices with their start and end apart: 3, of which 3 were waited for; matrix products, arithmetic and copies ran while one was open for 56% of the time, Pallas kernels for 0%

commit v1 on v0

--- a/solution.py
+++ b/solution.py
@@ -102,7 +102,9 @@
     attended = jnp.concatenate(attended_parts, axis=0)
     log_totals = jnp.concatenate(total_parts, axis=2)
     flat_out = attended.reshape(tree_len, heads_local * HEAD_SIZE)
-    shard_rows = lax.all_gather(cotangent, "ctx", axis=0, tiled=True)
+    shard_rows = jnp.concatenate(
+        lax.all_to_all(jnp.stack([cotangent] * lax.axis_size("ctx")), "ctx", 0, 0), axis=0
+    )
     weight_low = contract_rows(flat_out, shard_rows).astype(jnp.bfloat16)
     asking_heads = jnp.transpose(asking_matrix.reshape(tree_len, heads_local, HEAD_SIZE), (1, 0, 2))
     attended_heads = jnp.transpose(attended.reshape(tree_len, heads_local, HEAD_SIZE), (1, 0, 2))

time: 237 us -> 320 us (1.35)
  waiting for transfers between devices: 37.4 us -> 84.4 us
  blocking collectives: 27 us -> 57.2 us
  local copies, waits for them, and re-layouts: 43.5 us -> 49.9 us
    all_to_all x1, waiting for transfers between devices: 27.9 us -> 82.8 us  [local(): lax.all_to_all(jnp.stack([cotangent] * lax.axis_size('ctx')), 'ctx', 0, 0)]
    all_to_all x0 -> x1, blocking collectives: none -> 29.6 us  [local(): lax.all_to_all(query_key_value_rows, 'ctx', split_axis=1, concat_axis=0,...]
    all_gather x1 -> x0, waiting for transfers between devices: 6.48 us -> none  [local(): shard_rows = lax.all_gather(cotangent, 'ctx', axis=0, tiled=True)]
    another operation x2 -> x3, local copies, waits for them, and re-layouts: 0.07 us -> 5.33 us  [the longest x1 5.26 us: local(): jnp.stack([cotangent] * lax.axis_size('ctx'))]
    unnamed x13 -> x15, local copies, waits for them, and re-layouts: 15.4 us -> 15.4 us
  transfers between devices with their start and end apart: 3 -> 2, of which waited for: 3 -> 2; matrix products, arithmetic and copies ran while one was open for 56% -> 40% of each run, Pallas kernels for 0% -> 0%
where the time goes in v1:
time: 320 us; the launch traced here: 319 us
  matrix products  89.8 us (28%)
  waiting for transfers between devices  84.4 us (26%)
  blocking collectives  57.2 us (18%)
  local copies, waits for them, and re-layouts  49.9 us (16%)
  other arithmetic  16.4 us (5%)
  between operations  14.2 us (4%)
  starting transfers between devices  6.2 us (2%)
    all_to_all x1, waiting for transfers between devices, local(): lax.all_to_all(jnp.stack([cotangent] * lax.axis_size('ctx')), 'ctx', 0, 0)  82.8 us
    dot_general x21, matrix products, contract_cols(): lax.dot_general(left, right, (((1,), (1,)), ((), ())), preferred_element_...  39.6 us
    dot_general x21, matrix products, contract_rows(): lax.dot_general(left, right, (((0,), (0,)), ((), ())), preferred_element_...  38.2 us
    all_to_all x1, blocking collectives, local(): lax.all_to_all(query_key_value_rows, 'ctx', split_axis=1, concat_axis=0,...  29.6 us
    all_to_all x1, blocking collectives, local(): lax.all_to_all(gradients, 'ctx', split_axis=0, concat_axis=1, tiled=True)  27.6 us
    unnamed x15, local copies, waits for them, and re-layouts  15.4 us
    reduce_sum x5, other arithmetic, one_head(): jnp.sum(grad_rows.astype(jnp.float32) * own_rows.astype(jnp.float32), axi...  6.56 us
  transfers between devices with their start and end apart: 2, of which 2 were waited for; matrix products, arithmetic and copies ran while one was open for 40% of the time, Pallas kernels for 0%

profile of v1, /device:TPU:1, one launch (start us, length us, event | category | flops | bytes accessed | tf_op | source)
XLA Modules:
  0.0 318.7 jit_solution(4310144309406683412)
XLA Ops:
  7.2 3.9 %copy.59 = bf16[128,7168]{0,1:T(8,128)(2,1)} copy(bf16[128,7168]{1,0:T(8,128)(2,1)} %param.23) | data formatting | bytes 3670016 | tf_op args[0]
  11.0 29.6 %all_to_all.40 = bf16[128,8,896]{0,2,1:T(8,128)(2,1)S(1)} all-to-all(bf16[128,8,896]{0,2,1:T(8,128)(2,1)} %bitcast.313), channel_id=1, replica_groups=mesh['leaf'=16,'ctx'=8] {'ctx'}, dimensions={1} | all-to-all | bytes 3670016 | tf_op jit(solution)/shard_map/all_to_all | solution.py:57
  40.6 5.3 %stack.2 = bf16[8,128,5120]{2,1,0:T(8,128)(2,1)} broadcast(bf16[128,5120]{1,0:T(8,128)(2,1)S(1)} %copy-done.3), dimensions={1,2} | broadcast | bytes 11796480 | tf_op jit(solution)/shard_map/stack | solution.py:106
  45.9 6.2 %all-to-all-start.1 = ((bf16[8,128,5120]{2,1,0:T(8,128)(2,1)}), bf16[8,128,5120]{2,1,0:T(8,128)(2,1)}, u32[]{:S(2)}, u32[]{:S(2)}) async-start(bf16[8,128,5120]{2,1,0:T(8,128)(2,1)} %stack.2), calls=%async_computation.1 | async-start | bytes 20971520 | tf_op jit(solution)/shard_map/all_to_all | solution.py:106
  52.1 2.2 while.53
  60.8 2.4 copy.60
  63.2 2.9 reshape.562
  70.3 1.8 fusion.34
  72.2 2.2 exponential_reduce_fusion
  74.4 1.9 fusion.55
  76.3 3.7 %fusion.52 = bf16[512,1,5,128]{3,0,2,1:T(8,128)(2,1)S(1)} fusion(f32[1024,512,5]{1,0,2:T(8,128)S(1)} %get-tuple-element.624, f32[5,512]{1,0:T(8,128)S(1)} %log_add_fusion, f32[512]{0:T(512)S(1)} %get-tuple-element.622, pred[512,1024]{0,1:T(8,128)(4,1)S(1)} %copy-done.1, bf16[1024,1,7,128]{0,3,2,1:T(8,128)(2,1)S(1)} %reshape.562), kind=kOutput, calls=%fused_computation.85 | convolution fusion | flops 681902080 | bytes 11945984 | tf_op jit(solution)/shard_map/gjts,sgd->tgjd/dot_general | solution.py:94
  80.0 1.9 fusion.77
  81.9 2.5 copy.70
  85.6 82.8 %all-to-all-done.1 = bf16[8,128,5120]{2,1,0:T(8,128)(2,1)} async-done(((bf16[8,128,5120]{2,1,0:T(8,128)(2,1)}), bf16[8,128,5120]{2,1,0:T(8,128)(2,1)}, u32[]{:S(2)}, u32[]{:S(2)}) %all-to-all-start.1) | async-done | bytes 10485792 | tf_op jit(solution)/shard_map/all_to_all | solution.py:106
  168.4 11.7 %convolution_convert_fusion.3 = bf16[640,5120]{1,0:T(8,128)(2,1)} fusion(bf16[1024,640]{0,1:T(8,128)(2,1)} %bitcast.317, bf16[1024,5120]{1,0:T(8,128)(2,1)} %bitcast.54), kind=kOutput, calls=%fused_computation.66 | convolution fusion | flops 6714163200 | bytes 18350080 | tf_op jit(solution)/shard_map/dot_general | solution.py:44
  180.1 86.2 %conditional.1 = (bf16[1024,896]{0,1:T(8,128)(2,1)S(1)}) conditional(s32[]{:T(128)} %convert_element_type.154, () %tuple.93, (bf16[1024,5120]{1,0:T(8,128)(2,1)}, bf16[640,5120]{1,0:T(8,128)(2,1)}, f32[1,5,1024]{2,1,0:T(8,128)S(1)}, bf16[5,1024,128]{1,2,0:T(8,128)(2,1)}, bf16[1024,1,128]{2,0,1:T(8,128)(2,1)S(1)}, /*index=5*/f32[1024]{0:T(1024)S(1)}, ...), branch_computations={%region_7.8_spmd, %region_8.13_spmd} | conditional | flops 7727873024 | bytes 57315744 | solution.py:220
  180.1 11.6 %convolution_convert_fusion.2 = bf16[1024,640]{0,1:T(8,128)(2,1)S(1)} fusion(bf16[1024,5120]{1,0:T(8,128)(2,1)} %get-tuple-element.479, bf16[640,5120]{1,0:T(8,128)(2,1)} %get-tuple-element.510), kind=kOutput, calls=%fused_computation.54 | convolution fusion | flops 6711541760 | bytes 18350080 | tf_op jit(solution)/shard_map/cond/branch_1_fun/dot_general | solution.py:50
  193.3 70.4 %while.52 = (s32[]{:T(128)}, f32[1024,1,128]{2,0,1:T(8,128)S(1)}, f32[1024,1,128]{2,0,1:T(8,128)S(1)}, bf16[5,1024,128]{1,2,0:T(8,128)(2,1)}, bf16[5,1024,128]{1...) while((s32[]{:T(128)}, f32[1024,1,128]{2,0,1:T(8,128)S(1)}, ...), condition=%wide.region_12.12_spmd, body=%wide.region_9.11_spmd.sunk | while | flops 1014496256 | bytes 24809708 | solution.py:193
  228.4 1.6 subtract_exponential_fusion.2
  267.5 3.1 copy.72
  270.6 27.6 %all_to_all.41 = bf16[8,128,896]{2,1,0:T(8,128)(2,1)} all-to-all(bf16[8,128,896]{2,1,0:T(8,128)(2,1)S(1)} %bitcast.311), channel_id=1, replica_groups=mesh['leaf'=16,'ctx'=8] {'ctx'}, dimensions={0} | all-to-all | bytes 3670016 | tf_op jit(solution)/shard_map/all_to_all | solution.py:221
  298.2 3.2 copy.73
  301.4 2.9 copy.74
  305.8 6.1 %copy.127 = bf16[640,5120]{1,0:T(8,128)(2,1)} copy(bf16[640,5120]{1,0:T(8,128)(2,1)} %all-reduce.2.cloned.1.call-done) | data formatting | bytes 13107200
  (161 shorter events, 89.1 us)
Async XLA Ops:
  11.0 29.6 %copy-start.3 = (bf16[128,5120]{1,0:T(8,128)(2,1)S(1)}, bf16[128,5120]{1,0:T(8,128)(2,1)}, u32[]{:S(2)}) copy-start(bf16[128,5120]{1,0:T(8,128)(2,1)} %param.24) | copy-start | bytes 3932164
  45.9 6.2 %copy-start.5 = (s32[1,8]{1,0:T(1,128)S(1)}, s32[1,8]{1,0:T(1,128)}, u32[]{:S(2)}) copy-start(s32[1,8]{1,0:T(1,128)} %param.26) | copy-start | bytes 100
  45.9 122.5 %all-to-all-start.1 = ((bf16[8,128,5120]{2,1,0:T(8,128)(2,1)}), bf16[8,128,5120]{2,1,0:T(8,128)(2,1)}, u32[]{:S(2)}, u32[]{:S(2)}) async-start(bf16[8,128,5120]{2,1,0:T(8,128)(2,1)} %stack.2), calls=%async_computation.1 | async-start | bytes 20971520 | tf_op jit(solution)/shard_map/all_to_all | solution.py:106
  52.1 253.7 %all-reduce.2.cloned.1.call-start = ((), (), s32[]{:S(2)}) async-start(), calls=%async_computation.3 | async-start | bytes 13107200 | tf_op jit(solution)/shard_map/psum | solution.py:132
  54.3 6.5 %copy-start.4 = (s32[1024]{0:T(1024)S(1)}, s32[1024]{0:T(1024)}, u32[]{:S(2)}) copy-start(s32[1024]{0:T(1024)} %param.27) | copy-start | bytes 12292
  69.2 1.1 copy-start.1
  263.7 1.4 copy-start.2
  266.3 1.2 copy-start
Sparse Core Ops, SparseCore 0:
  180.2 125.4 all-reduce.1
